TPU v7x, 32 devices: a whole 2x2x4 slice. The times are simulated.
32 devices in a mesh: brick: 4 (over z), batch: 8 (over y, x, core).
Axes of the slice: x: 2, y: 2, z: 4, core: 2. Of those that a mesh axis runs over, the one named last changes fastest.
Arguments:
- coarse: bfloat16 [8, 4, 4, 8, 1024], P('batch', 'brick'), may hold values from -6 to 6
- coarse_mask: int32 [8, 4, 256], P('batch', 'brick'), may hold values 0 or 1
- skip: bfloat16 [8, 4, 8, 16, 1024], P('batch', 'brick'), may hold values from -6 to 6
- fine_mask: int32 [8, 4, 2048], P('batch', 'brick'), may hold values 0 or 1
- up_weight: bfloat16 [27, 64, 128], replicated, may hold values from -0.25 to 0.25
- fine_grad: bfloat16 [8, 4, 8, 16, 1024], P('batch', 'brick'), may hold values from -6 to 6
Outputs:
- fine_out: bfloat16 [8, 4, 8, 16, 1024], P('batch', 'brick')
- coarse_grad: bfloat16 [8, 4, 4, 8, 1024], P('batch', 'brick')
- weight_grad: float32 [27, 64, 128], replicated
All inputs are finite; a program needn't handle non-finite values. No bound on the sum of `coarse_mask` or of `fine_mask` on one device may be relied on, other than what follows from the above.
Results may differ from a plain program's by a relative error of at most 0.0035.
Values may be sent and summed in bfloat16 or wider, within the bound.
No kernel may reach another device: no remote copies, remote signals or barrier semaphores. Data moves between devices by JAX's collectives and lax.ppermute only.
A program may use at most 64 MiB of HBM per device.

v0:
```python
import math
import jax
import jax.numpy as jnp
from jax import lax
from jax.sharding import PartitionSpec as P

EVEN_TAPS = ((1, 0),)
ODD_TAPS = ((2, 0), (0, 1))
DIRECTIONS = ((1, 0, 0), (0, 1, 0), (0, 0, 1), (1, 1, 0), (1, 0, 1), (0, 1, 1), (1, 1, 1))
STRIDES = (4, 2, 1)


def from_behind(shard, axis, by):
    size = lax.axis_size(axis)
    pairs = [(i, i + by) for i in range(size) if 0 <= i + by < size]
    return lax.ppermute(shard, axis, pairs)


def tap_pairs(parity):
    if parity == 0:
        return EVEN_TAPS
    return ODD_TAPS


def spread(padded, weight):
    counts = (padded.shape[0] - 1, padded.shape[1] - 1, padded.shape[2] - 1)
    outputs = weight.shape[1]
    parts = []
    for parity_x in range(2):
        for parity_y in range(2):
            for parity_z in range(2):
                total = jnp.zeros(counts + (outputs,), jnp.float32)
                for tap_x, start_x in tap_pairs(parity_x):
                    for tap_y, start_y in tap_pairs(parity_y):
                        for tap_z, start_z in tap_pairs(parity_z):
                            window = padded[
                                start_x : start_x + counts[0],
                                start_y : start_y + counts[1],
                                start_z : start_z + counts[2],
                            ]
                            total = total + jnp.einsum(
                                "abci,oi->abco",
                                window,
                                weight[9 * tap_x + 3 * tap_y + tap_z],
                                preferred_element_type=jnp.float32,
                            )
                parts.append(total)
    stacked = jnp.stack(parts).reshape((2, 2, 2) + counts + (outputs,))
    return stacked.transpose(3, 0, 4, 1, 5, 2, 6).reshape(
        2 * counts[0], 2 * counts[1], 2 * counts[2], outputs
    )


def pick(field, tap, count, axis):
    return lax.slice_in_dim(field, tap, tap + 2 * count - 1, 2, axis)


def adjoint(widened, masked, weight):
    counts = masked.shape[:3]
    back = jnp.zeros(masked.shape, jnp.float32)
    grads = []
    for tap_x in range(3):
        along_x = pick(widened, tap_x, counts[0], 0)
        for tap_y in range(3):
            along_y = pick(along_x, tap_y, counts[1], 1)
            for tap_z in range(3):
                chosen = pick(along_y, tap_z, counts[2], 2)
                index = 9 * tap_x + 3 * tap_y + tap_z
                back = back + jnp.einsum(
                    "abco,oi->abci", chosen, weight[index], preferred_element_type=jnp.float32
                )
                grads.append(
                    jnp.einsum("abco,abci->oi", chosen, masked, preferred_element_type=jnp.float32)
                )
    return (back, jnp.stack(grads))


def offset(direction):
    return 4 * direction[0] + 2 * direction[1] + direction[2]


def allowed(direction, grid_y, grid_z, side):
    result = grid_y >= 0
    if direction[1]:
        result = result & (grid_y == side)
    if direction[2]:
        result = result & (grid_z == side)
    return result


def flatten(piece):
    return piece.reshape(piece.shape[0], -1)


def segment_index(other, axis, edge):
    if other < axis:
        return slice(1, None)
    if other > axis:
        return slice(None)
    return edge


def unit_of(axis):
    return tuple((1 if other == axis else 0 for other in range(3)))


def body(coarse, coarse_mask, skip, fine_mask, up_weight, fine_grad):
    rank = lax.axis_index("brick")
    grid_y = rank // 2 % 2
    grid_z = rank % 2
    size_x, size_y, merged = coarse.shape[2:]
    channels_out = up_weight.shape[1]
    channels_in = up_weight.shape[2]
    size_z = merged // channels_in
    fine_x, fine_y, fine_merged = skip.shape[2:]
    fine_z = fine_merged // channels_out
    coarse_keep = coarse_mask.reshape(size_x, size_y, size_z, 1).astype(jnp.bfloat16)
    masked = coarse.reshape(size_x, size_y, size_z, channels_in) * coarse_keep
    extended = spread(jnp.pad(masked, ((1, 1), (1, 1), (1, 1), (0, 0))), up_weight)[1:, 1:, 1:]
    for axis in range(3):
        source = tuple((segment_index(other, axis, slice(0, 1)) for other in range(3)))
        piece = extended[source]
        got = from_behind(flatten(piece).astype(jnp.bfloat16), "brick", -STRIDES[axis]).astype(
            jnp.float32
        )
        got = jnp.where(allowed(unit_of(axis), grid_y, grid_z, 0), got, 0.0).reshape(piece.shape)
        target = tuple((segment_index(other, axis, slice(-1, None)) for other in range(3)))
        extended = extended.at[target].add(got)
    up = extended[1:, 1:, 1:]
    fine_keep = fine_mask.reshape(fine_x, fine_y, fine_z, 1)
    fine = fine_keep.astype(jnp.float32) * (
        skip.reshape(fine_x, fine_y, fine_z, channels_out).astype(jnp.float32) + up
    )
    fine_out = fine.astype(jnp.bfloat16).reshape(skip.shape)
    cotangent = fine_grad.reshape(fine_x, fine_y, fine_z, channels_out) * fine_keep.astype(
        jnp.bfloat16
    )
    widened = jnp.pad(cotangent, ((1, 0), (1, 0), (1, 0), (0, 0)))
    for direction in DIRECTIONS:
        source = tuple((slice(-1, None) if flag else slice(None) for flag in direction))
        piece = cotangent[source]
        got = from_behind(flatten(piece), "brick", offset(direction))
        got = jnp.where(allowed(direction, grid_y, grid_z, 1), got, 0.0).reshape(piece.shape)
        target = tuple((slice(0, 1) if flag else slice(1, None) for flag in direction))
        widened = widened.at[target].set(got)
    back, grads = adjoint(widened, masked, up_weight)
    coarse_grad = (
        (back * coarse_keep.astype(jnp.float32)).astype(jnp.bfloat16).reshape(coarse.shape)
    )
    summed = lax.psum(grads, ("brick", "batch"))
    scale = 1.0 / math.sqrt(
        lax.axis_size("brick") * lax.axis_size("batch") * size_x * size_y * size_z
    )
    return (fine_out, coarse_grad, summed * scale)


def solution(mesh):
    in_specs = (
        P("batch", "brick", None, None, None),
        P("batch", "brick", None),
        P("batch", "brick", None, None, None),
        P("batch", "brick", None),
        P(),
        P("batch", "brick", None, None, None),
    )
    out_specs = (P("batch", "brick", None, None, None), P("batch", "brick", None, None, None), P())
    return jax.shard_map(body, mesh=mesh, in_specs=in_specs, out_specs=out_specs, check_vma=False)
```

profile of v0, /device:TPU:0, one launch (start us, length us, event | category | flops | bytes accessed | tf_op | source)
XLA Modules:
  0.0 260.1 jit_solution(2375744965565836065)
XLA Ops:
  11.3 5.9 %collective-permute-start.4 = (bf16[8,1024]{1,0:T(8,128)(2,1)S(1)}, bf16[8,1024]{1,0:T(8,128)(2,1)S(1)}, u32[]{:S(2)}, u32[]{:S(2)}) collective-permute-start(bf16[8,1024]{1,0:T(8,128)(2,1)S(1)} %reshape.526), channel_id=1, source_target_pairs={{0,16},{8,24},{1,17},{9,25},{2,18},{10,26},{3,19},{11,27},{4,20},{... | collective-permute-start | bytes 49160 | tf_op jit(solution)/shard_map/ppermute | solution.py:16
  17.6 3.5 %collective-permute-start.5 = (bf16[8,1024]{1,0:T(8,128)(2,1)S(1)}, bf16[8,1024]{1,0:T(8,128)(2,1)S(1)}, u32[]{:S(2)}, u32[]{:S(2)}) collective-permute-start(bf16[8,1024]{1,0:T(8,128)(2,1)S(1)} %reshape.528), channel_id=1, source_target_pairs={{0,8},{8,16},{16,24},{1,9},{9,17},{17,25},{2,10},{10,18},{18,26},{... | collective-permute-start | bytes 49160 | tf_op jit(solution)/shard_map/ppermute | solution.py:16
  31.6 2.0 copy.82
  33.7 2.4 reshape.518
  39.8 2.2 reshape.539
  63.2 2.4 fusion.190
  65.6 2.8 %slice.746 = bf16[4,8,8,64]{3,2,1,0:T(8,128)(2,1)} slice(bf16[4,8,17,64]{3,2,1,0:T(8,128)(2,1)} %get-tuple-element.135), slice={[0:4:1], [0:8:1], [0:15:2], [0:64:1]} | slice | bytes 65536 | tf_op jit(solution)/shard_map/slice | solution.py:55
  68.4 2.8 %slice.747 = bf16[4,8,8,64]{3,2,1,0:T(8,128)(2,1)} slice(bf16[4,8,17,64]{3,2,1,0:T(8,128)(2,1)} %get-tuple-element.135), slice={[0:4:1], [0:8:1], [1:16:2], [0:64:1]} | slice | bytes 65536 | tf_op jit(solution)/shard_map/slice | solution.py:55
  71.1 2.8 %slice.748 = bf16[4,8,8,64]{3,2,1,0:T(8,128)(2,1)} slice(bf16[4,8,17,64]{3,2,1,0:T(8,128)(2,1)} %get-tuple-element.135), slice={[0:4:1], [0:8:1], [2:17:2], [0:64:1]} | slice | bytes 65536 | tf_op jit(solution)/shard_map/slice | solution.py:55
  74.0 2.8 %slice.750 = bf16[4,8,8,64]{3,2,1,0:T(8,128)(2,1)} slice(bf16[4,8,17,64]{3,2,1,0:T(8,128)(2,1)} %get-tuple-element.136), slice={[0:4:1], [0:8:1], [0:15:2], [0:64:1]} | slice | bytes 65536 | tf_op jit(solution)/shard_map/slice | solution.py:55
  76.7 2.7 %slice.751 = bf16[4,8,8,64]{3,2,1,0:T(8,128)(2,1)} slice(bf16[4,8,17,64]{3,2,1,0:T(8,128)(2,1)} %get-tuple-element.136), slice={[0:4:1], [0:8:1], [1:16:2], [0:64:1]} | slice | bytes 65536 | tf_op jit(solution)/shard_map/slice | solution.py:55
  79.5 2.8 %slice.752 = bf16[4,8,8,64]{3,2,1,0:T(8,128)(2,1)} slice(bf16[4,8,17,64]{3,2,1,0:T(8,128)(2,1)} %get-tuple-element.136), slice={[0:4:1], [0:8:1], [2:17:2], [0:64:1]} | slice | bytes 65536 | tf_op jit(solution)/shard_map/slice | solution.py:55
  91.1 1.7 fusion.43
  93.9 1.7 fusion.42
  95.6 1.7 fusion.41
  97.3 1.7 fusion.40
  98.9 1.7 fusion.39
  138.3 1.7 fusion.48
  145.1 4.1 %collective-permute-done.1 = bf16[8,1088]{1,0:T(8,128)(2,1)S(1)} collective-permute-done((bf16[8,1088]{1,0:T(8,128)(2,1)S(1)}, bf16[8,1088]{1,0:T(8,128)(2,1)S(1)}, u32[]{:S(2)}, u32[]{:S(2)}) %collective-permute-start.1) | collective-permute-done | bytes 17440 | tf_op jit(solution)/shard_map/ppermute | solution.py:16
  155.1 2.8 %collective-permute-done.2 = bf16[8,1024]{1,0:T(8,128)(2,1)S(1)} collective-permute-done((bf16[8,1024]{1,0:T(8,128)(2,1)S(1)}, bf16[8,1024]{1,0:T(8,128)(2,1)S(1)}, u32[]{:S(2)}, u32[]{:S(2)}) %collective-permute-start.2) | collective-permute-done | bytes 16416 | tf_op jit(solution)/shard_map/ppermute | solution.py:16
  159.1 3.0 %scatter-add.14 = f32[9,17,17,64]{3,2,1,0:T(8,128)} dynamic-update-slice(f32[9,17,17,64]{3,2,1,0:T(8,128)} %fusion.47, f32[8,16,1,64]{3,2,1,0:T(1,128)S(1)} %slice_add_fusion.3, s32[]{:T(128)} %constant.355.clone.1, s32[]{:T(128)} %constant.355.clone.1, s32[]{:T(128)} %constant.361.clone.1, s32[]{:T(128)} %constant.356.clone.1) | dynamic-update-slice | bytes 65540 | tf_op jit(solution)/shard_map/scatter-add | solution.py:128
  162.1 1.7 fusion.45
  164.9 86.2 %all-reduce.4.cloned.1.call-done = f32[27,64,128]{2,1,0:T(8,128)} async-done(((f32[27,64,128]{2,1,0:T(8,128)}), f32[27,64,128]{2,1,0:T(8,128)}) %all-reduce.4.cloned.1.call-update) | async-done | bytes 884752 | tf_op jit(solution)/shard_map/psum | solution.py:150
  251.1 2.2 broadcast_multiply_fusion
  (248 shorter events, 99.8 us)
Async XLA Ops:
  7.2 18.2 %copy-start.2 = (bf16[27,64,128]{2,1,0:T(8,128)(2,1)S(1)}, bf16[27,64,128]{2,1,0:T(8,128)(2,1)}, u32[]{:S(2)}) copy-start(bf16[27,64,128]{2,1,0:T(8,128)(2,1)} %param.30) | copy-start | bytes 1327108
  7.2 243.9 %all-reduce.4.cloned.1.call-start = ((), (), s32[]{:S(2)}) async-start(), calls=%async_computation | async-start | bytes 1769472 | tf_op jit(solution)/shard_map/psum | solution.py:150
  9.8 17.7 %copy-start.1 = (bf16[8,16,16,64]{3,2,1,0:T(8,128)(2,1)}, bf16[8,16,16,64]{3,2,1,0:T(8,128)(2,1)S(1)}, u32[]{:S(2)}) copy-start(bf16[8,16,16,64]{3,2,1,0:T(8,128)(2,1)S(1)} %broadcast_multiply_fusion.1) | copy-start | bytes 786436
  10.6 37.2 %collective-permute-start.3 = (bf16[1,16384]{1,0:T(2,128)(2,1)}, bf16[1,16384]{1,0:T(2,128)(2,1)S(1)}, u32[]{:S(2)}, u32[]{:S(2)}) collective-permute-start(bf16[1,16384]{1,0:T(2,128)(2,1)} %reshape.524), channel_id=1, source_target_pairs={} | collective-permute-start | bytes 98312 | tf_op jit(solution)/shard_map/ppermute | solution.py:16
  11.3 36.1 %collective-permute-start.4 = (bf16[8,1024]{1,0:T(8,128)(2,1)S(1)}, bf16[8,1024]{1,0:T(8,128)(2,1)S(1)}, u32[]{:S(2)}, u32[]{:S(2)}) collective-permute-start(bf16[8,1024]{1,0:T(8,128)(2,1)S(1)} %reshape.526), channel_id=1, source_target_pairs={{0,16},{8,24},{1,17},{9,25},{2,18},{10,26},{3,19},{11,27},{4,20},{... | collective-permute-start | bytes 49160 | tf_op jit(solution)/shard_map/ppermute | solution.py:16
  17.6 29.9 %collective-permute-start.5 = (bf16[8,1024]{1,0:T(8,128)(2,1)S(1)}, bf16[8,1024]{1,0:T(8,128)(2,1)S(1)}, u32[]{:S(2)}, u32[]{:S(2)}) collective-permute-start(bf16[8,1024]{1,0:T(8,128)(2,1)S(1)} %reshape.528), channel_id=1, source_target_pairs={{0,8},{8,16},{16,24},{1,9},{9,17},{17,25},{2,10},{10,18},{18,26},{... | collective-permute-start | bytes 49160 | tf_op jit(solution)/shard_map/ppermute | solution.py:16
  21.2 24.8 %collective-permute-start.6 = (bf16[1,1024]{1,0:T(2,128)(2,1)S(1)}, bf16[1,1024]{1,0:T(2,128)(2,1)S(1)}, u32[]{:S(2)}, u32[]{:S(2)}) collective-permute-start(bf16[1,1024]{1,0:T(2,128)(2,1)S(1)} %reshape.530), channel_id=1, source_target_pairs={} | collective-permute-start | bytes 6152 | tf_op jit(solution)/shard_map/ppermute | solution.py:16
  21.9 20.8 %collective-permute-start.9 = (bf16[1,64]{1,0:T(2,128)(2,1)S(1)}, bf16[1,64]{1,0:T(2,128)(2,1)S(1)}, u32[]{:S(2)}, u32[]{:S(2)}) collective-permute-start(bf16[1,64]{1,0:T(2,128)(2,1)S(1)} %slice_bitcast_fusion), channel_id=1, source_target_pairs={} | collective-permute-start | bytes 392 | tf_op jit(solution)/shard_map/ppermute | solution.py:16
  42.7 2.6 collective-permute-start.8
  45.3 2.0 collective-permute-start.7
  46.0 92.3 %collective-permute-start = (bf16[1,18496]{1,0:T(2,128)(2,1)}, bf16[1,18496]{1,0:T(2,128)(2,1)}, u32[]{:S(2)}, u32[]{:S(2)}) collective-permute-start(bf16[1,18496]{1,0:T(2,128)(2,1)} %convert_element_type.107), channel_id=1, source_target_pairs={} | collective-permute-start | bytes 110984 | tf_op jit(solution)/shard_map/ppermute | solution.py:16
  56.8 36.1 %copy-start.3 = (bf16[27,64,128]{2,1,0:T(8,128)(2,1)S(1)}, bf16[27,64,128]{2,1,0:T(8,128)(2,1)}, u32[]{:S(2)}) copy-start(bf16[27,64,128]{2,1,0:T(8,128)(2,1)} %param.30) | copy-start | bytes 1327108
  90.2 25.3 %copy-start.7 = (bf16[4,8,8,64]{3,2,1,0:T(8,128)(2,1)}, bf16[4,8,8,64]{3,2,1,0:T(8,128)(2,1)S(1)}, u32[]{:S(2)}) copy-start(bf16[4,8,8,64]{3,2,1,0:T(8,128)(2,1)S(1)} %slice.763) | copy-start | bytes 98308
  90.9 27.8 %copy-start.6 = (bf16[4,8,8,64]{3,2,1,0:T(8,128)(2,1)}, bf16[4,8,8,64]{3,2,1,0:T(8,128)(2,1)S(1)}, u32[]{:S(2)}) copy-start(bf16[4,8,8,64]{3,2,1,0:T(8,128)(2,1)S(1)} %slice.768) | copy-start | bytes 98308
  91.1 28.4 %copy-start.4 = (bf16[4,8,8,64]{3,2,1,0:T(8,128)(2,1)}, bf16[4,8,8,64]{3,2,1,0:T(8,128)(2,1)S(1)}, u32[]{:S(2)}) copy-start(bf16[4,8,8,64]{3,2,1,0:T(8,128)(2,1)S(1)} %slice.769) | copy-start | bytes 98308
  91.1 12.8 %copy-start.33 = (bf16[4,8,8,64]{3,2,1,0:T(8,128)(2,1)S(1)}, bf16[4,8,8,64]{3,2,1,0:T(8,128)(2,1)}, u32[]{:S(2)}) copy-start(bf16[4,8,8,64]{3,2,1,0:T(8,128)(2,1)} %slice.746) | copy-start | bytes 98308
  91.1 16.9 %copy-start.32 = (bf16[4,8,8,64]{3,2,1,0:T(8,128)(2,1)S(1)}, bf16[4,8,8,64]{3,2,1,0:T(8,128)(2,1)}, u32[]{:S(2)}) copy-start(bf16[4,8,8,64]{3,2,1,0:T(8,128)(2,1)} %slice.750) | copy-start | bytes 98308
  92.9 16.0 %copy-start.27 = (bf16[4,8,8,64]{3,2,1,0:T(8,128)(2,1)S(1)}, bf16[4,8,8,64]{3,2,1,0:T(8,128)(2,1)}, u32[]{:S(2)}) copy-start(bf16[4,8,8,64]{3,2,1,0:T(8,128)(2,1)} %slice.751) | copy-start | bytes 98308
  95.6 14.1 %copy-start.23 = (bf16[4,8,8,64]{3,2,1,0:T(8,128)(2,1)S(1)}, bf16[4,8,8,64]{3,2,1,0:T(8,128)(2,1)}, u32[]{:S(2)}) copy-start(bf16[4,8,8,64]{3,2,1,0:T(8,128)(2,1)} %slice.752) | copy-start | bytes 98308
  97.3 13.3 %copy-start.19 = (bf16[4,8,8,64]{3,2,1,0:T(8,128)(2,1)S(1)}, bf16[4,8,8,64]{3,2,1,0:T(8,128)(2,1)}, u32[]{:S(2)}) copy-start(bf16[4,8,8,64]{3,2,1,0:T(8,128)(2,1)} %slice.754) | copy-start | bytes 98308
  130.1 23.4 %copy-start.5 = (bf16[4,8,8,64]{3,2,1,0:T(8,128)(2,1)S(1)}, bf16[4,8,8,64]{3,2,1,0:T(8,128)(2,1)}, u32[]{:S(2)}) copy-start(bf16[4,8,8,64]{3,2,1,0:T(8,128)(2,1)} %copy-done.4) | copy-start | bytes 98308
  130.6 31.5 %copy-start = (f32[8,16,16,64]{3,2,1,0:T(8,128)S(1)}, f32[8,16,16,64]{3,2,1,0:T(8,128)}, u32[]{:S(2)}) copy-start(f32[8,16,16,64]{3,2,1,0:T(8,128)} %reshape.539) | copy-start | bytes 1572868
  142.7 6.5 %collective-permute-start.1 = (bf16[8,1088]{1,0:T(8,128)(2,1)S(1)}, bf16[8,1088]{1,0:T(8,128)(2,1)S(1)}, u32[]{:S(2)}, u32[]{:S(2)}) collective-permute-start(bf16[8,1088]{1,0:T(8,128)(2,1)S(1)} %convert_element_type.109), channel_id=1, source_target_pairs={{16,0},{24,8},{17,1},{25,9},{18,2},{26,10},{19,3},{27,11},{20,4},{... | collective-permute-start | bytes 52232 | tf_op jit(solution)/shard_map/ppermute | solution.py:16
  152.2 5.6 %collective-permute-start.2 = (bf16[8,1024]{1,0:T(8,128)(2,1)S(1)}, bf16[8,1024]{1,0:T(8,128)(2,1)S(1)}, u32[]{:S(2)}, u32[]{:S(2)}) collective-permute-start(bf16[8,1024]{1,0:T(8,128)(2,1)S(1)} %convert_element_type.111), channel_id=1, source_target_pairs={{8,0},{16,8},{24,16},{9,1},{17,9},{25,17},{10,2},{18,10},{26,18},{... | collective-permute-start | bytes 49160 | tf_op jit(solution)/shard_map/ppermute | solution.py:16
  (22 other events, 230.7 us)
Sparse Core Ops, SparseCore 0:
  120.5 130.5 all-reduce.3
where the time goes:
time: 263 us; the launch traced here: 260 us
  waiting for transfers between devices  94.5 us (36%)
  local copies, waits for them, and re-layouts  65.6 us (25%)
  matrix products  55.9 us (21%)
  starting transfers between devices  17.2 us (7%)
  between operations  14.9 us (6%)
  other arithmetic  12.1 us (5%)
    psum x1, waiting for transfers between devices, body(): summed = lax.psum(grads, ('brick', 'batch'))  86.2 us
    slice x30, local copies, waits for them, and re-layouts, pick(): return lax.slice_in_dim(field, tap, tap + 2 * count - 1, 2, axis)  40.5 us
    dot_general x27, matrix products, adjoint(): jnp.einsum('abco,abci->oi', chosen, masked, preferred_element_type=jnp.fl...  28.1 us
    dot_general x27, matrix products, adjoint(): jnp.einsum('abco,oi->abci', chosen, weight[index], preferred_element_type...  20.8 us
    ppermute x10, starting transfers between devices, from_behind(): return lax.ppermute(shard, axis, pairs)  17.2 us
    ppermute x10, waiting for transfers between devices, from_behind(): return lax.ppermute(shard, axis, pairs)  8.22 us
    dot_general x27, matrix products, spread(): jnp.einsum('abci,oi->abco', window, weight[9 * tap_x + 3 * tap_y + tap_z]...  7.06 us
  transfers between devices with their start and end apart: 11, of which 4 were waited for; matrix products, arithmetic and copies ran while one was open for 49% of the time, Pallas kernels for 0%

commit v1 on v0

--- a/solution.py
+++ b/solution.py
@@ -147,7 +147,7 @@
     coarse_grad = (
         (back * coarse_keep.astype(jnp.float32)).astype(jnp.bfloat16).reshape(coarse.shape)
     )
-    summed = lax.psum(grads, ("brick", "batch"))
+    summed = jnp.sum(lax.all_gather(grads, ("brick", "batch")), axis=0)
     scale = 1.0 / math.sqrt(
         lax.axis_size("brick") * lax.axis_size("batch") * size_x * size_y * size_z
     )

time: 263 us -> 233 us (0.89)
  local copies, waits for them, and re-layouts: 65.6 us -> 26.9 us
  waiting for transfers between devices: 94.5 us -> 126 us
  matrix products: 55.9 us -> 26 us
  other arithmetic: 12.1 us -> 20.3 us
    all_gather x0 -> x1, waiting for transfers between devices: none -> 117 us  [body(): summed = jnp.sum(lax.all_gather(grads, ('brick', 'batch')), axis=0)]
    psum x1 -> x0, waiting for transfers between devices: 86.2 us -> none  [body(): summed = lax.psum(grads, ('brick', 'batch'))]
    slice x30, local copies, waits for them, and re-layouts: 40.5 us -> 5.18 us  [pick(): return lax.slice_in_dim(field, tap, tap + 2 * count - 1, 2, axis)]
    dot_general x27, matrix products: 28.1 us -> 5.29 us  [adjoint(): jnp.einsum('abco,abci->oi', chosen, masked, preferred_element_type=jnp.fl...]
    reduce_sum x0 -> x1, other arithmetic: none -> 10.2 us  [body(): summed = jnp.sum(lax.all_gather(grads, ('brick', 'batch')), axis=0)]
    dot_general x27, matrix products: 20.8 us -> 14.3 us  [adjoint(): jnp.einsum('abco,oi->abci', chosen, weight[index], preferred_element_type...]
  transfers between devices with their start and end apart: 11 -> 11, of which waited for: 4 -> 4; matrix products, arithmetic and copies ran while one was open for 49% -> 19% of each run, Pallas kernels for 0% -> 0%
where the time goes in v1:
time: 233 us; the launch traced here: 232 us
  waiting for transfers between devices  126 us (54%)
  local copies, waits for them, and re-layouts  26.9 us (12%)
  matrix products  26 us (11%)
  other arithmetic  20.3 us (9%)
  starting transfers between devices  17.2 us (7%)
  between operations  15.7 us (7%)
    all_gather x1, waiting for transfers between devices, body(): summed = jnp.sum(lax.all_gather(grads, ('brick', 'batch')), axis=0)  117 us
    ppermute x10, starting transfers between devices, from_behind(): return lax.ppermute(shard, axis, pairs)  17.2 us
    dot_general x27, matrix products, adjoint(): jnp.einsum('abco,oi->abci', chosen, weight[index], preferred_element_type...  14.3 us
    reduce_sum x1, other arithmetic, body(): summed = jnp.sum(lax.all_gather(grads, ('brick', 'batch')), axis=0)  10.2 us
    ppermute x10, waiting for transfers between devices, from_behind(): return lax.ppermute(shard, axis, pairs)  8.41 us
    dot_general x27, matrix products, spread(): jnp.einsum('abci,oi->abco', window, weight[9 * tap_x + 3 * tap_y + tap_z]...  6.35 us
    dot_general x27, matrix products, adjoint(): jnp.einsum('abco,abci->oi', chosen, masked, preferred_element_type=jnp.fl...  5.29 us
    slice x30, local copies, waits for them, and re-layouts, pick(): return lax.slice_in_dim(field, tap, tap + 2 * count - 1, 2, axis)  5.18 us
  transfers between devices with their start and end apart: 11, of which 4 were waited for; matrix products, arithmetic and copies ran while one was open for 19% of the time, Pallas kernels for 0%

profile of v1, /device:TPU:0, one launch (start us, length us, event | category | flops | bytes accessed | tf_op | source)
XLA Modules:
  0.0 231.7 jit_solution(2063388781603478803)
XLA Ops:
  7.2 1.3 reshape.523
  10.6 5.9 %collective-permute-start.4 = (bf16[8,1024]{1,0:T(8,128)(2,1)S(1)}, bf16[8,1024]{1,0:T(8,128)(2,1)S(1)}, u32[]{:S(2)}, u32[]{:S(2)}) collective-permute-start(bf16[8,1024]{1,0:T(8,128)(2,1)S(1)} %reshape.526), channel_id=1, source_target_pairs={{0,16},{8,24},{1,17},{9,25},{2,18},{10,26},{3,19},{11,27},{4,20},{... | collective-permute-start | bytes 49160 | tf_op jit(solution)/shard_map/ppermute | solution.py:16
  16.9 3.5 %collective-permute-start.5 = (bf16[8,1024]{1,0:T(8,128)(2,1)S(1)}, bf16[8,1024]{1,0:T(8,128)(2,1)S(1)}, u32[]{:S(2)}, u32[]{:S(2)}) collective-permute-start(bf16[8,1024]{1,0:T(8,128)(2,1)S(1)} %reshape.528), channel_id=1, source_target_pairs={{0,8},{8,16},{16,24},{1,9},{9,17},{17,25},{2,10},{10,18},{18,26},{... | collective-permute-start | bytes 49160 | tf_op jit(solution)/shard_map/ppermute | solution.py:16
  23.2 1.3 collective-permute-start.8
  24.5 1.3 collective-permute-done.8
  27.7 1.4 scatter.26
  48.6 2.1 copy.88
  50.7 2.5 %reshape.518 = f32[10,18,18,64]{3,2,1,0:T(8,128)S(1)} reshape(f32[5,2,9,2,9,2,64]{6,5,4,3,2,1,0:T(2,128)} %bitcast.610) | data formatting | bytes 1658880 | tf_op jit(solution)/shard_map/reshape | solution.py:49
  54.0 1.3 collective-permute-start
  55.3 1.5 slice.770
  70.9 1.1 fusion.48
  73.8 1.3 collective-permute-start.1
  75.1 1.1 convolution_add_fusion.20
  76.2 4.1 %collective-permute-done.1 = bf16[8,1088]{1,0:T(8,128)(2,1)S(1)} collective-permute-done((bf16[8,1088]{1,0:T(8,128)(2,1)S(1)}, bf16[8,1088]{1,0:T(8,128)(2,1)S(1)}, u32[]{:S(2)}, u32[]{:S(2)}) %collective-permute-start.1) | collective-permute-done | bytes 17440 | tf_op jit(solution)/shard_map/ppermute | solution.py:16
  80.5 1.6 fusion.47
  82.1 1.3 fusion.50
  83.4 1.3 collective-permute-start.2
  86.4 3.0 %collective-permute-done.2 = bf16[8,1024]{1,0:T(8,128)(2,1)S(1)} collective-permute-done((bf16[8,1024]{1,0:T(8,128)(2,1)S(1)}, bf16[8,1024]{1,0:T(8,128)(2,1)S(1)}, u32[]{:S(2)}, u32[]{:S(2)}) %collective-permute-start.2) | collective-permute-done | bytes 16416 | tf_op jit(solution)/shard_map/ppermute | solution.py:16
  89.5 1.1 slice_add_fusion.3
  90.6 3.0 %scatter-add.14 = f32[9,17,17,64]{3,2,1,0:T(8,128)} dynamic-update-slice(f32[9,17,17,64]{3,2,1,0:T(8,128)} %fusion.47, f32[8,16,1,64]{3,2,1,0:T(1,128)S(1)} %slice_add_fusion.3, s32[]{:T(128)} %constant.355.clone.1, s32[]{:T(128)} %constant.355.clone.1, s32[]{:T(128)} %constant.361.clone.1, s32[]{:T(128)} %constant.356.clone.1) | dynamic-update-slice | bytes 65540 | tf_op jit(solution)/shard_map/scatter-add | solution.py:128
  93.6 1.7 fusion.45
  95.4 1.1 reshape.522
  96.4 117.3 %all-gather.3.cloned.1.call-done = f32[864,64,128]{2,1,0:T(8,128)} async-done(((f32[27,64,128]{2,1,0:T(8,128)}), f32[864,64,128]{2,1,0:T(8,128)}) %all-gather.3.cloned.1.call-update) | async-done | bytes 28311568 | tf_op jit(solution)/shard_map/all_gather | solution.py:150
  213.7 10.2 %reduce_sum.9 = f32[27,64,128]{2,1,0:T(8,128)S(1)} reduce(f32[32,27,64,128]{3,2,1,0:T(8,128)} %bitcast.609, f32[]{:T(128)} %constant.359.clone.1), dimensions={0}, to_apply=%region_0.1 | reduce | flops 6856704 | bytes 29196292 | tf_op jit(solution)/shard_map/reduce_sum | solution.py:150
  (277 shorter events, 44.8 us)
Async XLA Ops:
  7.2 15.9 %copy-start.47 = (bf16[1,1,4,8,1024]{4,3,2,1,0:T(8,128)(2,1)S(1)}, bf16[1,1,4,8,1024]{4,3,2,1,0:T(8,128)(2,1)}, u32[]{:S(2)}) copy-start(bf16[1,1,4,8,1024]{4,3,2,1,0:T(8,128)(2,1)} %param.26) | copy-start | bytes 196612
  7.2 206.5 %all-gather.3.cloned.1.call-start = ((), (), s32[]{:S(2)}) async-start(), calls=%async_computation | async-start | bytes 29196288 | tf_op jit(solution)/shard_map/all_gather | solution.py:150
  9.8 17.1 %collective-permute-start.3 = (bf16[1,16384]{1,0:T(2,128)(2,1)S(1)}, bf16[1,16384]{1,0:T(2,128)(2,1)S(1)}, u32[]{:S(2)}, u32[]{:S(2)}) collective-permute-start(bf16[1,16384]{1,0:T(2,128)(2,1)S(1)} %reshape.524), channel_id=1, source_target_pairs={} | collective-permute-start | bytes 98312 | tf_op jit(solution)/shard_map/ppermute | solution.py:16
  10.6 16.1 %collective-permute-start.4 = (bf16[8,1024]{1,0:T(8,128)(2,1)S(1)}, bf16[8,1024]{1,0:T(8,128)(2,1)S(1)}, u32[]{:S(2)}, u32[]{:S(2)}) collective-permute-start(bf16[8,1024]{1,0:T(8,128)(2,1)S(1)} %reshape.526), channel_id=1, source_target_pairs={{0,16},{8,24},{1,17},{9,25},{2,18},{10,26},{3,19},{11,27},{4,20},{... | collective-permute-start | bytes 49160 | tf_op jit(solution)/shard_map/ppermute | solution.py:16
  16.9 9.8 %collective-permute-start.5 = (bf16[8,1024]{1,0:T(8,128)(2,1)S(1)}, bf16[8,1024]{1,0:T(8,128)(2,1)S(1)}, u32[]{:S(2)}, u32[]{:S(2)}) collective-permute-start(bf16[8,1024]{1,0:T(8,128)(2,1)S(1)} %reshape.528), channel_id=1, source_target_pairs={{0,8},{8,16},{16,24},{1,9},{9,17},{17,25},{2,10},{10,18},{18,26},{... | collective-permute-start | bytes 49160 | tf_op jit(solution)/shard_map/ppermute | solution.py:16
  20.5 6.0 %collective-permute-start.6 = (bf16[1,1024]{1,0:T(2,128)(2,1)S(1)}, bf16[1,1024]{1,0:T(2,128)(2,1)S(1)}, u32[]{:S(2)}, u32[]{:S(2)}) collective-permute-start(bf16[1,1024]{1,0:T(2,128)(2,1)S(1)} %reshape.530), channel_id=1, source_target_pairs={} | collective-permute-start | bytes 6152 | tf_op jit(solution)/shard_map/ppermute | solution.py:16
  21.1 2.0 collective-permute-start.9
  23.2 2.6 %collective-permute-start.8 = (bf16[8,64]{1,0:T(8,128)(2,1)S(1)}, bf16[8,64]{1,0:T(8,128)(2,1)S(1)}, u32[]{:S(2)}, u32[]{:S(2)}) collective-permute-start(bf16[8,64]{1,0:T(8,128)(2,1)S(1)} %bitcast.614), channel_id=1, source_target_pairs={{0,24},{1,25},{2,26},{3,27},{4,28},{5,29},{6,30},{7,31}} | collective-permute-start | bytes 3080 | tf_op jit(solution)/shard_map/ppermute | solution.py:16
  25.8 0.7 collective-permute-start.7
  54.0 16.9 %collective-permute-start = (bf16[1,18496]{1,0:T(2,128)(2,1)}, bf16[1,18496]{1,0:T(2,128)(2,1)}, u32[]{:S(2)}, u32[]{:S(2)}) collective-permute-start(bf16[1,18496]{1,0:T(2,128)(2,1)} %convert_element_type.107), channel_id=1, source_target_pairs={} | collective-permute-start | bytes 110984 | tf_op jit(solution)/shard_map/ppermute | solution.py:16
  57.7 10.8 %copy-start.29 = (bf16[4,8,8,64]{3,2,1,0:T(8,128)(2,1)S(1)}, bf16[4,8,8,64]{3,2,1,0:T(8,128)(2,1)}, u32[]{:S(2)}) copy-start(bf16[4,8,8,64]{3,2,1,0:T(8,128)(2,1)} %copy-done.28) | copy-start | bytes 98308
  57.7 11.0 %copy-start.26 = (bf16[4,8,8,64]{3,2,1,0:T(8,128)(2,1)S(1)}, bf16[4,8,8,64]{3,2,1,0:T(8,128)(2,1)}, u32[]{:S(2)}) copy-start(bf16[4,8,8,64]{3,2,1,0:T(8,128)(2,1)} %copy-done.25) | copy-start | bytes 98308
  57.7 11.1 %copy-start.24 = (bf16[4,8,8,64]{3,2,1,0:T(8,128)(2,1)S(1)}, bf16[4,8,8,64]{3,2,1,0:T(8,128)(2,1)}, u32[]{:S(2)}) copy-start(bf16[4,8,8,64]{3,2,1,0:T(8,128)(2,1)} %copy-done.23) | copy-start | bytes 98308
  57.7 11.3 %copy-start.22 = (bf16[4,8,8,64]{3,2,1,0:T(8,128)(2,1)S(1)}, bf16[4,8,8,64]{3,2,1,0:T(8,128)(2,1)}, u32[]{:S(2)}) copy-start(bf16[4,8,8,64]{3,2,1,0:T(8,128)(2,1)} %copy-done.21) | copy-start | bytes 98308
  58.5 9.3 %copy-start.1 = (bf16[27,64,128]{2,1,0:T(8,128)(2,1)S(1)}, bf16[27,64,128]{2,1,0:T(8,128)(2,1)}, u32[]{:S(2)}) copy-start(bf16[27,64,128]{2,1,0:T(8,128)(2,1)} %param.30) | copy-start | bytes 1327108
  58.5 9.3 %copy-start.45 = (bf16[4,8,8,64]{3,2,1,0:T(8,128)(2,1)S(1)}, bf16[4,8,8,64]{3,2,1,0:T(8,128)(2,1)}, u32[]{:S(2)}) copy-start(bf16[4,8,8,64]{3,2,1,0:T(8,128)(2,1)} %copy-done.44) | copy-start | bytes 98308
  58.5 9.4 %copy-start.41 = (bf16[4,8,8,64]{3,2,1,0:T(8,128)(2,1)S(1)}, bf16[4,8,8,64]{3,2,1,0:T(8,128)(2,1)}, u32[]{:S(2)}) copy-start(bf16[4,8,8,64]{3,2,1,0:T(8,128)(2,1)} %copy-done.40) | copy-start | bytes 98308
  58.5 9.6 %copy-start.38 = (bf16[4,8,8,64]{3,2,1,0:T(8,128)(2,1)S(1)}, bf16[4,8,8,64]{3,2,1,0:T(8,128)(2,1)}, u32[]{:S(2)}) copy-start(bf16[4,8,8,64]{3,2,1,0:T(8,128)(2,1)} %copy-done.37) | copy-start | bytes 98308
  58.5 9.7 %copy-start.36 = (bf16[4,8,8,64]{3,2,1,0:T(8,128)(2,1)S(1)}, bf16[4,8,8,64]{3,2,1,0:T(8,128)(2,1)}, u32[]{:S(2)}) copy-start(bf16[4,8,8,64]{3,2,1,0:T(8,128)(2,1)} %copy-done.35) | copy-start | bytes 98308
  58.5 9.9 %copy-start.32 = (bf16[4,8,8,64]{3,2,1,0:T(8,128)(2,1)S(1)}, bf16[4,8,8,64]{3,2,1,0:T(8,128)(2,1)}, u32[]{:S(2)}) copy-start(bf16[4,8,8,64]{3,2,1,0:T(8,128)(2,1)} %copy-done.31) | copy-start | bytes 98308
  59.6 9.6 %copy-start.20 = (bf16[4,8,8,64]{3,2,1,0:T(8,128)(2,1)S(1)}, bf16[4,8,8,64]{3,2,1,0:T(8,128)(2,1)}, u32[]{:S(2)}) copy-start(bf16[4,8,8,64]{3,2,1,0:T(8,128)(2,1)} %copy-done.19) | copy-start | bytes 98308
  60.6 8.7 %copy-start.18 = (bf16[4,8,8,64]{3,2,1,0:T(8,128)(2,1)S(1)}, bf16[4,8,8,64]{3,2,1,0:T(8,128)(2,1)}, u32[]{:S(2)}) copy-start(bf16[4,8,8,64]{3,2,1,0:T(8,128)(2,1)} %copy-done.17) | copy-start | bytes 98308
  73.8 6.5 %collective-permute-start.1 = (bf16[8,1088]{1,0:T(8,128)(2,1)S(1)}, bf16[8,1088]{1,0:T(8,128)(2,1)S(1)}, u32[]{:S(2)}, u32[]{:S(2)}) collective-permute-start(bf16[8,1088]{1,0:T(8,128)(2,1)S(1)} %convert_element_type.109), channel_id=1, source_target_pairs={{16,0},{24,8},{17,1},{25,9},{18,2},{26,10},{19,3},{27,11},{20,4},{... | collective-permute-start | bytes 52232 | tf_op jit(solution)/shard_map/ppermute | solution.py:16
  83.4 6.0 %collective-permute-start.2 = (bf16[8,1024]{1,0:T(8,128)(2,1)S(1)}, bf16[8,1024]{1,0:T(8,128)(2,1)S(1)}, u32[]{:S(2)}, u32[]{:S(2)}) collective-permute-start(bf16[8,1024]{1,0:T(8,128)(2,1)S(1)} %convert_element_type.111), channel_id=1, source_target_pairs={{8,0},{16,8},{24,16},{9,1},{17,9},{25,17},{10,2},{18,10},{26,18},{... | collective-permute-start | bytes 49160 | tf_op jit(solution)/shard_map/ppermute | solution.py:16
  (36 other events, 188.4 us)
Sparse Core Ops, SparseCore 0:
  42.2 171.4 all-gather.2
